TPU v7x, 512 devices: a whole 4x4x16 slice. The times are simulated.
512 devices in a mesh: rep: 32 (over z, core), row: 4 (over x), col: 4 (over y).
Axes of the slice: x: 4, y: 4, z: 16, core: 2. Of those that a mesh axis runs over, the one named last changes fastest.
Arguments:
- coordinates: bfloat16 [128, 32, 3, 128], P('rep')
- resample: int32 [32, 22], P('rep'), may hold values from 0 to 127, as said below
- block_slot: int32 [128], replicated, may hold values from 0 to 127, as said below
- lag_time: int32 [32], P('rep'), may hold values from 1 to 8
- atom_pairs: int32 [2, 4096], replicated, may hold values from 0 to 127, as said below
Outputs:
- instant_cov: bfloat16 [32, 4096, 4096], P('rep', 'row', 'col')
- lagged_cov: bfloat16 [32, 4096, 4096], P('rep', 'row', 'col')
Inputs may be any that keep to these rules, and one draw needn't show every extreme that they name: `resample`: the owner of a block is block_slot // 4. In each replicate at most 2 draws have one owner, and some owner has exactly 2; a block may be drawn more than once. `block_slot`: each slot holds exactly one block. `atom_pairs`: the two atoms of a feature differ, and no unordered pair of atoms appears twice.
All inputs are finite; a program needn't handle non-finite values.
Results may differ from a plain program's by a relative error of at most 0.0073.
Values may be sent and summed in bfloat16 or wider, within the bound.
No kernel may reach another device: no remote copies, remote signals or barrier semaphores. Data moves between devices by JAX's collectives and lax.ppermute only.
A program may use at most 64 MiB of HBM per device.

v0:
```python
import jax
import jax.numpy as jnp
from jax import lax
from jax.sharding import PartitionSpec as P

F = 4096
ATOMS = 128
BLOCK_LEN = 32
DRAWS = 22


def slot_lookup(lists, slot_table):
    matches = lists[..., None] == jnp.arange(slot_table.shape[0], dtype=jnp.int32)
    return jnp.sum(jnp.where(matches, slot_table, 0), axis=-1)


def owner_rank(lists, slot_table, blk_count):
    slots = slot_lookup(lists, slot_table)
    owner_ids = slots // blk_count
    local_ids = slots % blk_count
    draw_ids = jnp.arange(lists.shape[-1], dtype=jnp.int32)
    before = (owner_ids[..., :, None] == owner_ids[..., None, :]) & (
        draw_ids[None, :] < draw_ids[:, None]
    )
    ranks = jnp.sum(before.astype(jnp.int32), axis=-1)
    return (owner_ids, local_ids, ranks)


def pack_requests(resample, block_slot, local_data, capacity):
    every_list = lax.all_gather(resample, "rep", axis=0, tiled=True)
    blk_count = local_data.shape[0]
    owners_all, local_all, ranks_all = owner_rank(every_list, block_slot, blk_count)
    myself = lax.axis_index("rep")
    wanted = (owners_all == myself)[:, :, None] & (
        ranks_all[:, :, None] == jnp.arange(capacity, dtype=jnp.int32)
    )
    picked = local_all[:, :, None] == jnp.arange(blk_count, dtype=jnp.int32)
    selector = jnp.einsum(
        "rdc,rdk->rck", wanted.astype(jnp.float32), picked.astype(jnp.float32)
    ).astype(jnp.bfloat16)
    return jnp.einsum(
        "rck,kx->rcx", selector, local_data, preferred_element_type=jnp.float32
    ).astype(jnp.bfloat16)


def unpack_blocks(received, resample, block_slot, blk_count, capacity):
    owner_ids, local_ids, ranks = owner_rank(resample[0], block_slot, blk_count)
    rows_wanted = owner_ids * capacity + ranks
    flat = received.reshape(-1, received.shape[-1])
    return jnp.take(flat, rows_wanted, axis=0)


def tile_features(chosen, atom_pairs, first_feature, width, shift):
    first_atoms = lax.dynamic_slice_in_dim(atom_pairs[0], first_feature, width)
    second_atoms = lax.dynamic_slice_in_dim(atom_pairs[1], first_feature, width)
    atom_ids = jnp.arange(chosen.shape[-1], dtype=jnp.int32)[:, None]
    signed = (
        (atom_ids == first_atoms[None, :]).astype(jnp.float32)
        - (atom_ids == second_atoms[None, :]).astype(jnp.float32)
    ).astype(jnp.bfloat16)
    flat = chosen.reshape(-1, chosen.shape[-1])
    difference = jnp.dot(flat, signed, preferred_element_type=jnp.float32).reshape(
        DRAWS, BLOCK_LEN, 3, width
    )
    squared = (
        difference[:, :, 0] * difference[:, :, 0]
        + difference[:, :, 1] * difference[:, :, 1]
        + difference[:, :, 2] * difference[:, :, 2]
    )
    features = jnp.sqrt(squared).astype(jnp.bfloat16)
    doubled = jnp.concatenate([features, features], axis=1)
    shifted = lax.dynamic_slice_in_dim(doubled, shift, BLOCK_LEN, axis=1)
    valid_rows = (jnp.arange(BLOCK_LEN, dtype=jnp.int32) < BLOCK_LEN - shift)[None, :, None]
    pair_count = (2 * DRAWS * (BLOCK_LEN - shift)).astype(jnp.float32)
    earlier = jnp.where(valid_rows, features.astype(jnp.float32), 0.0)
    later = jnp.where(valid_rows, shifted.astype(jnp.float32), 0.0)
    feature_mean = (jnp.sum(earlier, axis=(0, 1)) + jnp.sum(later, axis=(0, 1))) / pair_count
    zero_lag = (
        jnp.where(valid_rows, earlier - feature_mean, 0.0).astype(jnp.bfloat16).reshape(-1, width)
    )
    lagged = (
        jnp.where(valid_rows, later - feature_mean, 0.0).astype(jnp.bfloat16).reshape(-1, width)
    )
    return (zero_lag, lagged, pair_count)


def shards(coordinates, resample, block_slot, lag_time, atom_pairs):
    rep_total = lax.axis_size("rep")
    per_owner = (DRAWS + rep_total - 1) // rep_total
    capacity = max(2, per_owner + per_owner // 2)
    blk_count = coordinates.shape[0]
    outgoing = pack_requests(resample, block_slot, coordinates.reshape(blk_count, -1), capacity)
    received = lax.all_to_all(outgoing, "rep", split_axis=0, concat_axis=0, tiled=True)
    chosen = unpack_blocks(received, resample, block_slot, blk_count, capacity).reshape(
        DRAWS, BLOCK_LEN, 3, ATOMS
    )
    width = F // lax.axis_size("row")
    shift = lag_time[0]
    zero_row, lag_row, pair_count = tile_features(
        chosen, atom_pairs, lax.axis_index("row") * width, width, shift
    )
    row_stack = jnp.concatenate([zero_row, lag_row], axis=0)
    zero_col, lag_col, unused_count = tile_features(
        chosen, atom_pairs, lax.axis_index("col") * width, width, shift
    )
    col_stack = jnp.concatenate([zero_col, lag_col], axis=0)
    half_rows = col_stack.shape[0] // 2
    mirrored = jnp.concatenate([col_stack[half_rows:], col_stack[:half_rows]], axis=0)
    instant = (
        jnp.einsum("na,nb->ab", row_stack, col_stack, preferred_element_type=jnp.float32)
        / pair_count
    )
    crossed = (
        jnp.einsum("na,nb->ab", row_stack, mirrored, preferred_element_type=jnp.float32)
        / pair_count
    )
    return (instant[None].astype(jnp.bfloat16), crossed[None].astype(jnp.bfloat16))


def solution(mesh):
    return jax.shard_map(
        shards,
        mesh=mesh,
        in_specs=(P("rep", None, None, None), P("rep", None), P(), P("rep"), P()),
        out_specs=(P("rep", "row", "col"), P("rep", "row", "col")),
        check_vma=False,
    )
```

profile of v0, /device:TPU:1, one launch (start us, length us, event | category | flops | bytes accessed | tf_op | source)
XLA Modules:
  0.0 158.3 jit_solution(3388728040057878747)
XLA Ops:
  0.7 37.5 %all-gather = s32[32,1,22]{2,1,0:T(1,128)S(1)} all-gather(s32[1,1,22]{2,1,0:T(1,128)} %bitcast.64), channel_id=1, replica_groups=mesh['rep'=32,'row'=4,'col'=4] {'rep'}, dimensions={0}, use_global_device_ids=true | all-gather | bytes 2904 | tf_op jit(solution)/shard_map/all_gather | solution.py:30
  38.2 0.1 copy.26
  38.3 1.2 select_reduce_fusion.2
  39.5 0.2 convert_reduce_fusion
  39.7 0.1 copy.28
  39.8 0.1 copy.27
  39.9 0.1 copy.29
  40.0 1.0 copy.30
  40.9 0.1 reshape.274
  41.0 0.2 convolution_convert_fusion.1
  41.2 0.5 convolution_convert_fusion
  41.8 2.8 %copy.32 = bf16[32,2,12288]{2,1,0:T(2,128)(2,1)} copy(bf16[32,2,12288]{2,0,1:T(8,128)(2,1)S(1)} %convolution_convert_fusion) | data formatting | bytes 3145728 | tf_op jit(solution)/shard_map/convert_element_type | solution.py:43
  44.5 7.0 %all-to-all-start = ((bf16[32,2,12288]{2,1,0:T(2,128)(2,1)}), bf16[32,2,12288]{2,1,0:T(2,128)(2,1)S(1)}, u32[]{:S(2)}, u32[]{:S(2)}) async-start(bf16[32,2,12288]{2,1,0:T(2,128)(2,1)} %copy.32), calls=%async_computation | async-start | bytes 3145728 | tf_op jit(solution)/shard_map/all_to_all | solution.py:93
  52.2 0.1 broadcast_in_dim.106
  52.3 0.2 select_reduce_fusion.3
  52.5 0.2 convert_reduce_fusion.1
  52.8 76.7 %all-to-all-done = bf16[32,2,12288]{2,1,0:T(2,128)(2,1)S(1)} async-done(((bf16[32,2,12288]{2,1,0:T(2,128)(2,1)}), bf16[32,2,12288]{2,1,0:T(2,128)(2,1)S(1)}, u32[]{:S(2)}, u32[]{:S(2)}) %all-to-all-start) | async-done | bytes 1572896 | tf_op jit(solution)/shard_map/all_to_all | solution.py:93
  129.5 0.6 reshape.259
  130.1 0.9 gather_fusion
  131.0 0.8 gather.7
  131.8 0.4 broadcast_select_fusion
  132.2 1.3 fusion.32
  133.5 1.2 fusion.56
  134.8 1.2 fusion.2
  136.0 1.3 fusion.34
  137.3 1.2 fusion.57
  138.5 1.2 fusion.6
  139.7 5.3 %fusion.23 = (f32[1024]{0:T(1024)S(1)}, f32[1024]{0:T(1024)S(1)}, f32[1024]{0:T(1024)S(1)}, f32[1024]{0:T(1024)S(1)}) fusion(pred[32]{0:T(512)(128)(4,1)S(1)} %iota_compare_fusion.9, s32[]{:T(128)S(6)} %select_n.137, bf16[22,32,1024]{2,1,0:T(8,128)(2,1)S(1)} %fusion.57, bf16[22,32,1024]{2,1,0:T(8,128)(2,1)S(1)} %fusion.56, ...), kind=kLoop, calls=%fused_computation.45 | loop fusion | flops 21622784 | bytes 20201508 | tf_op jit(solution)/shard_map/reduce_sum | solution.py:77
  145.0 2.6 %select_convert_fusion.1 = (bf16[22,32,1024]{2,1,0:T(8,128)(2,1)S(1)}, bf16[22,32,1024]{2,1,0:T(8,128)(2,1)S(1)}) fusion(f32[1024]{0:T(1024)S(1)} %get-tuple-element.19, pred[32]{0:T(512)(128)(4,1)S(1)} %iota_compare_fusion.9, s32[]{:T(128)S(6)} %select_n.137, bf16[22,32,1024]{2,1,0:T(8,128)(2,1)S(1)} %fusion.57, f32[1024]{0:T(1024)S(1)} %get-tuple-element.18, ...), kind=kLoop, calls=%fused_computation.43 | loop fusion | flops 11534336 | bytes 5775396 | tf_op jit(solution)/shard_map/convert_element_type | solution.py:82
  147.6 1.4 fusion.21
  149.0 4.7 %fusion.25 = bf16[1,1024,1024]{2,1,0:T(8,128)(2,1)} fusion(f32[]{:T(128)S(6)} %convert_element_type.94, bf16[704,1024]{1,0:T(8,128)(2,1)S(1)} %get-tuple-element.15, bf16[704,1024]{1,0:T(8,128)(2,1)S(1)} %bitcast.57, bf16[704,1024]{1,0:T(8,128)(2,1)S(1)} %bitcast.55, bf16[704,1024]{1,0:T(8,128)(2,1)S(1)} %get-tuple-element.14), kind=kOutput, calls=%fused_computation.48 | convolution fusion | flops 2966421504 | bytes 7864324 | tf_op jit(solution)/shard_map/na,nb->ab/dot_general | solution.py:114
  153.7 4.6 %fusion.24 = bf16[1,1024,1024]{2,1,0:T(8,128)(2,1)} fusion(f32[]{:T(128)S(6)} %convert_element_type.94, bf16[704,1024]{1,0:T(8,128)(2,1)S(1)} %bitcast.58, bf16[704,1024]{1,0:T(8,128)(2,1)S(1)} %get-tuple-element.15, bf16[704,1024]{1,0:T(8,128)(2,1)S(1)} %bitcast.56, bf16[704,1024]{1,0:T(8,128)(2,1)S(1)} %get-tuple-element.14), kind=kOutput, calls=%fused_computation.47 | convolution fusion | flops 2966421504 | bytes 7864324 | tf_op jit(solution)/shard_map/na,nb->ab/dot_general | solution.py:110
  (19 shorter events, 0.2 us)
Async XLA Ops:
  41.7 10.6 %copy-start.1 = (s32[128]{0:T(128)S(1)}, s32[128]{0:T(128)}, u32[]{:S(2)}) copy-start(s32[128]{0:T(128)} %param.7) | copy-start | bytes 1540
  41.8 10.6 %copy-start.2 = (s32[1,22]{1,0:T(1,128)S(1)}, s32[1,22]{1,0:T(1,128)}, u32[]{:S(2)}) copy-start(s32[1,22]{1,0:T(1,128)} %param.6) | copy-start | bytes 268
  41.8 11.0 %copy-start = (s32[2,4096]{1,0:T(2,128)S(1)}, s32[2,4096]{1,0:T(2,128)}, u32[]{:S(2)}) copy-start(s32[2,4096]{1,0:T(2,128)} %param.9) | copy-start | bytes 98308
  44.5 85.0 %all-to-all-start = ((bf16[32,2,12288]{2,1,0:T(2,128)(2,1)}), bf16[32,2,12288]{2,1,0:T(2,128)(2,1)S(1)}, u32[]{:S(2)}, u32[]{:S(2)}) async-start(bf16[32,2,12288]{2,1,0:T(2,128)(2,1)} %copy.32), calls=%async_computation | async-start | bytes 3145728 | tf_op jit(solution)/shard_map/all_to_all | solution.py:93
where the time goes:
time: 159 us; the launch traced here: 158 us
  waiting for transfers between devices  76.7 us (48%)
  blocking collectives  37.5 us (24%)
  other arithmetic  16.4 us (10%)
  matrix products  12.6 us (8%)
  starting transfers between devices  6.98 us (4%)
  local copies, waits for them, and re-layouts  6.61 us (4%)
    all_to_all x1, waiting for transfers between devices, shards(): lax.all_to_all(outgoing, 'rep', split_axis=0, concat_axis=0, tiled=True)  76.7 us
    all_gather x1, blocking collectives, pack_requests(): every_list = lax.all_gather(resample, 'rep', axis=0, tiled=True)  37.5 us
    all_to_all x1, starting transfers between devices, shards(): lax.all_to_all(outgoing, 'rep', split_axis=0, concat_axis=0, tiled=True)  6.98 us
    reduce_sum x1, other arithmetic, tile_features(): jnp.sum(later, axis=(0, 1))  5.29 us
    dot_general x1, matrix products, shards(): jnp.einsum('na,nb->ab', row_stack, mirrored, preferred_element_type=jnp.f...  4.66 us
    dot_general x1, matrix products, shards(): jnp.einsum('na,nb->ab', row_stack, col_stack, preferred_element_type=jnp....  4.65 us
  transfers between devices with their start and end apart: 1, of which 1 were waited for; matrix products, arithmetic and copies ran while one was open for 0% of the time, Pallas kernels for 0%

commit v1 on v0

--- a/solution.py
+++ b/solution.py
@@ -27,7 +27,9 @@
 
 
 def pack_requests(resample, block_slot, local_data, capacity):
-    every_list = lax.all_gather(resample, "rep", axis=0, tiled=True)
+    every_list = jnp.concatenate(
+        lax.all_to_all(jnp.stack([resample] * lax.axis_size("rep")), "rep", 0, 0), axis=0
+    )
     blk_count = local_data.shape[0]
     owners_all, local_all, ranks_all = owner_rank(every_list, block_slot, blk_count)
     myself = lax.axis_index("rep")

time: 159 us -> 147 us (0.925)
  blocking collectives: 37.5 us -> 0 us
  starting transfers between devices: 6.98 us -> 21.3 us
  waiting for transfers between devices: 76.7 us -> 87.4 us
    all_gather x1 -> x0, blocking collectives: 37.5 us -> none  [pack_requests(): every_list = lax.all_gather(resample, 'rep', axis=0, tiled=True)]
    all_to_all x0 -> x1, starting transfers between devices: none -> 16.7 us  [pack_requests(): lax.all_to_all(jnp.stack([resample] * lax.axis_size('rep')), 'rep', 0, 0)]
    all_to_all x0 -> x1, waiting for transfers between devices: none -> 10.6 us  [pack_requests(): lax.all_to_all(jnp.stack([resample] * lax.axis_size('rep')), 'rep', 0, 0)]
    all_to_all x1, starting transfers between devices: 6.98 us -> 4.54 us  [shards(): lax.all_to_all(outgoing, 'rep', split_axis=0, concat_axis=0, tiled=True)]
  transfers between devices with their start and end apart: 1 -> 2, of which waited for: 1 -> 2; matrix products, arithmetic and copies ran while one was open for 0% -> 1% of each run, Pallas kernels for 0% -> 0%
where the time goes in v1:
time: 147 us
  waiting for transfers between devices  87.4 us (59%)
  starting transfers between devices  21.3 us (14%)
  other arithmetic  16.4 us (11%)
  matrix products  12.6 us (9%)
  local copies, waits for them, and re-layouts  7.89 us (5%)
  between operations  1.54 us (1%)
    all_to_all x1, waiting for transfers between devices, shards(): lax.all_to_all(outgoing, 'rep', split_axis=0, concat_axis=0, tiled=True)  76.7 us
    all_to_all x1, starting transfers between devices, pack_requests(): lax.all_to_all(jnp.stack([resample] * lax.axis_size('rep')), 'rep', 0, 0)  16.7 us
    all_to_all x1, waiting for transfers between devices, pack_requests(): lax.all_to_all(jnp.stack([resample] * lax.axis_size('rep')), 'rep', 0, 0)  10.6 us
    reduce_sum x1, other arithmetic, tile_features(): jnp.sum(later, axis=(0, 1))  5.29 us
    dot_general x1, matrix products, shards(): jnp.einsum('na,nb->ab', row_stack, mirrored, preferred_element_type=jnp.f...  4.66 us
    dot_general x1, matrix products, shards(): jnp.einsum('na,nb->ab', row_stack, col_stack, preferred_element_type=jnp....  4.65 us
    all_to_all x1, starting transfers between devices, shards(): lax.all_to_all(outgoing, 'rep', split_axis=0, concat_axis=0, tiled=True)  4.54 us
  transfers between devices with their start and end apart: 2, of which 2 were waited for; matrix products, arithmetic and copies ran while one was open for 1% of the time, Pallas kernels for 0%

profile of v1, /device:TPU:1, one launch (start us, length us, event | category | flops | bytes accessed | tf_op | source)
XLA Modules:
  0.0 147.1 jit_solution(7988762982760921713)
XLA Ops:
  0.6 1.3 stack.2
  1.9 16.7 %all-to-all-start = ((s32[32,1,22]{2,1,0:T(1,128)}), s32[32,1,22]{2,1,0:T(1,128)S(1)}, u32[]{:S(2)}, u32[]{:S(2)}) async-start(s32[32,1,22]{2,1,0:T(1,128)} %stack.2), calls=%async_computation | async-start | bytes 32768 | tf_op jit(solution)/shard_map/all_to_all | solution.py:31
  18.7 1.0 copy.41
  19.6 0.1 reshape.275
  19.7 10.6 %all-to-all-done = s32[32,1,22]{2,1,0:T(1,128)S(1)} async-done(((s32[32,1,22]{2,1,0:T(1,128)}), s32[32,1,22]{2,1,0:T(1,128)S(1)}, u32[]{:S(2)}, u32[]{:S(2)}) %all-to-all-start) | async-done | bytes 2848 | tf_op jit(solution)/shard_map/all_to_all | solution.py:31
  30.5 1.2 select_reduce_fusion.2
  31.7 0.2 convert_reduce_fusion
  31.9 0.1 copy.39
  32.0 0.1 copy.38
  32.2 0.2 convolution_convert_fusion.1
  32.3 0.5 convolution_convert_fusion
  32.9 2.8 %copy.43 = bf16[32,2,12288]{2,1,0:T(2,128)(2,1)} copy(bf16[32,2,12288]{2,0,1:T(8,128)(2,1)S(1)} %convolution_convert_fusion) | data formatting | bytes 3145728 | tf_op jit(solution)/shard_map/convert_element_type | solution.py:45
  35.7 4.5 %all-to-all-start.1 = ((bf16[32,2,12288]{2,1,0:T(2,128)(2,1)}), bf16[32,2,12288]{2,1,0:T(2,128)(2,1)S(1)}, u32[]{:S(2)}, u32[]{:S(2)}) async-start(bf16[32,2,12288]{2,1,0:T(2,128)(2,1)} %copy.43), calls=%async_computation.1 | async-start | bytes 3145728 | tf_op jit(solution)/shard_map/all_to_all | solution.py:95
  40.9 0.1 broadcast_in_dim.105
  41.0 0.2 select_reduce_fusion.3
  41.2 0.2 convert_reduce_fusion.1
  41.5 76.7 %all-to-all-done.1 = bf16[32,2,12288]{2,1,0:T(2,128)(2,1)S(1)} async-done(((bf16[32,2,12288]{2,1,0:T(2,128)(2,1)}), bf16[32,2,12288]{2,1,0:T(2,128)(2,1)S(1)}, u32[]{:S(2)}, u32[]{:S(2)}) %all-to-all-start.1) | async-done | bytes 1572896 | tf_op jit(solution)/shard_map/all_to_all | solution.py:95
  118.3 0.6 reshape.262
  118.9 0.9 gather_fusion
  119.8 0.8 gather.7
  120.6 0.4 broadcast_select_fusion
  121.0 1.3 fusion.32
  122.3 1.2 fusion.56
  123.5 1.2 fusion.2
  124.7 1.3 fusion.34
  126.0 1.2 fusion.57
  127.3 1.2 fusion.6
  128.5 5.3 %fusion.23 = (f32[1024]{0:T(1024)S(1)}, f32[1024]{0:T(1024)S(1)}, f32[1024]{0:T(1024)S(1)}, f32[1024]{0:T(1024)S(1)}) fusion(pred[32]{0:T(512)(128)(4,1)S(1)} %iota_compare_fusion.9, s32[]{:T(128)S(6)} %select_n.137, bf16[22,32,1024]{2,1,0:T(8,128)(2,1)S(1)} %fusion.57, bf16[22,32,1024]{2,1,0:T(8,128)(2,1)S(1)} %fusion.56, ...), kind=kLoop, calls=%fused_computation.45 | loop fusion | flops 21622784 | bytes 20201508 | tf_op jit(solution)/shard_map/reduce_sum | solution.py:79
  133.8 2.6 %select_convert_fusion.1 = (bf16[22,32,1024]{2,1,0:T(8,128)(2,1)S(1)}, bf16[22,32,1024]{2,1,0:T(8,128)(2,1)S(1)}) fusion(f32[1024]{0:T(1024)S(1)} %get-tuple-element.19, pred[32]{0:T(512)(128)(4,1)S(1)} %iota_compare_fusion.9, s32[]{:T(128)S(6)} %select_n.137, bf16[22,32,1024]{2,1,0:T(8,128)(2,1)S(1)} %fusion.57, f32[1024]{0:T(1024)S(1)} %get-tuple-element.18, ...), kind=kLoop, calls=%fused_computation.43 | loop fusion | flops 11534336 | bytes 5775396 | tf_op jit(solution)/shard_map/convert_element_type | solution.py:84
  136.4 1.4 fusion.21
  137.8 4.7 %fusion.25 = bf16[1,1024,1024]{2,1,0:T(8,128)(2,1)} fusion(f32[]{:T(128)S(6)} %convert_element_type.94, bf16[704,1024]{1,0:T(8,128)(2,1)S(1)} %get-tuple-element.15, bf16[704,1024]{1,0:T(8,128)(2,1)S(1)} %bitcast.56, bf16[704,1024]{1,0:T(8,128)(2,1)S(1)} %bitcast.54, bf16[704,1024]{1,0:T(8,128)(2,1)S(1)} %get-tuple-element.14), kind=kOutput, calls=%fused_computation.48 | convolution fusion | flops 2966421504 | bytes 7864324 | tf_op jit(solution)/shard_map/na,nb->ab/dot_general | solution.py:116
  142.5 4.6 %fusion.24 = bf16[1,1024,1024]{2,1,0:T(8,128)(2,1)} fusion(f32[]{:T(128)S(6)} %convert_element_type.94, bf16[704,1024]{1,0:T(8,128)(2,1)S(1)} %bitcast.57, bf16[704,1024]{1,0:T(8,128)(2,1)S(1)} %get-tuple-element.15, bf16[704,1024]{1,0:T(8,128)(2,1)S(1)} %bitcast.55, bf16[704,1024]{1,0:T(8,128)(2,1)S(1)} %get-tuple-element.14), kind=kOutput, calls=%fused_computation.47 | convolution fusion | flops 2966421504 | bytes 7864324 | tf_op jit(solution)/shard_map/na,nb->ab/dot_general | solution.py:112
  (21 shorter events, 0.3 us)
Async XLA Ops:
  1.9 28.5 %all-to-all-start = ((s32[32,1,22]{2,1,0:T(1,128)}), s32[32,1,22]{2,1,0:T(1,128)S(1)}, u32[]{:S(2)}, u32[]{:S(2)}) async-start(s32[32,1,22]{2,1,0:T(1,128)} %stack.2), calls=%async_computation | async-start | bytes 32768 | tf_op jit(solution)/shard_map/all_to_all | solution.py:31
  32.9 8.1 %copy-start.1 = (s32[128]{0:T(128)S(1)}, s32[128]{0:T(128)}, u32[]{:S(2)}) copy-start(s32[128]{0:T(128)} %param.7) | copy-start | bytes 1540
  32.9 8.1 %copy-start.2 = (s32[1,22]{1,0:T(1,128)S(1)}, s32[1,22]{1,0:T(1,128)}, u32[]{:S(2)}) copy-start(s32[1,22]{1,0:T(1,128)} %param.6) | copy-start | bytes 268
  32.9 8.5 %copy-start = (s32[2,4096]{1,0:T(2,128)S(1)}, s32[2,4096]{1,0:T(2,128)}, u32[]{:S(2)}) copy-start(s32[2,4096]{1,0:T(2,128)} %param.9) | copy-start | bytes 98308
  35.7 82.6 %all-to-all-start.1 = ((bf16[32,2,12288]{2,1,0:T(2,128)(2,1)}), bf16[32,2,12288]{2,1,0:T(2,128)(2,1)S(1)}, u32[]{:S(2)}, u32[]{:S(2)}) async-start(bf16[32,2,12288]{2,1,0:T(2,128)(2,1)} %copy.43), calls=%async_computation.1 | async-start | bytes 3145728 | tf_op jit(solution)/shard_map/all_to_all | solution.py:95
